TPU v7x, 32 devices: a whole 2x2x4 slice. The times are simulated.
32 devices in a mesh: sub: 8 (over z, x), grp: 4 (over y, core).
Axes of the slice: x: 2, y: 2, z: 4, core: 2. Of those that a mesh axis runs over, the one named last changes fastest.
Arguments:
- resid: float32 [32768, 256], P(('sub', 'grp')), may hold values from -6 to 6
- schur_inv: bfloat16 [65536, 2048], P(('sub', 'grp')), may hold values from -0.125 to 0.125
- basis: bfloat16 [512, 2048], P(('sub', 'grp')), may hold values from -1.5 to 1.5
- scaling: float32 [65536], P(('sub', 'grp')), may hold values from 0.25 to 1
- coarse_inv: bfloat16 [512, 512], P(('sub', 'grp')), may hold values from -0.5 to 0.5
- source_row: int32 [65536], P(('sub', 'grp')), may hold values from 0 to 3071, as said below
- primal_idx: int32 [512], P(('sub', 'grp')), may hold values from 0 to 2047, as said below
Outputs:
- first_apply: float32 [32768, 256], P(('sub', 'grp'))
- second_apply: float32 [32768, 256], P(('sub', 'grp'))
Inputs may be any that keep to these rules, and one draw needn't show every extreme that they name: `source_row`: within one subdomain the entries are distinct; the first subdomain of each chain has none below 1024, the last none at or above 2048. `primal_idx`: within one subdomain the entries are distinct.
All inputs are finite; a program needn't handle non-finite values.
Results may differ from a plain program's by a relative error of at most 0.0076.
Values may be sent and summed in bfloat16 or wider, within the bound.
No kernel may reach another device: no remote copies, remote signals or barrier semaphores. Data moves between devices by JAX's collectives and lax.ppermute only.
A program may use at most 64 MiB of HBM per device.

v0:
```python
import jax
import jax.numpy as jnp
from jax import lax
from jax.sharding import PartitionSpec as P


def with_halo(cells, sides, width):
    for axis, dim in sides:
        count = lax.axis_size(axis)
        ends = count - 1
        head = lax.slice_in_dim(cells, 0, width, axis=dim)
        tail = lax.slice_in_dim(cells, cells.shape[dim] - width, cells.shape[dim], axis=dim)
        cells = jnp.concatenate(
            [
                lax.ppermute(tail, axis, [(i, (i + 1) % count) for i in range(ends)]),
                cells,
                lax.ppermute(head, axis, [((i + 1) % count, i) for i in range(ends)]),
            ],
            axis=dim,
        )
    return cells


def shifted(shard, axis, by):
    devices = lax.axis_size(axis)
    pairs = [(i, i + by) for i in range(devices) if 0 <= i + by < devices]
    return lax.ppermute(shard, axis, pairs)


def shards(resid, schur_inv, basis, scaling, coarse_inv, source_row, primal_idx):
    own_count = resid.shape[0]
    scale_column = scaling[:, None]

    def add_all(portion):
        return jnp.dot(coarse_inv, portion, preferred_element_type=jnp.float32)

    def precondition(vector_in):
        rounded = vector_in.astype(jnp.bfloat16)
        padded = with_halo(rounded, (("sub", 0),), own_count)
        gathered = padded[source_row]
        scaled = (scale_column * gathered.astype(jnp.float32)).astype(jnp.bfloat16)
        primal = scaled[primal_idx]
        coarse = add_all(lax.all_gather(primal, ("sub", "grp"), axis=0, tiled=True))
        coarse_rounded = coarse.astype(jnp.bfloat16)
        solved = jnp.dot(schur_inv, scaled, preferred_element_type=jnp.float32)
        solved = solved + lax.dot_general(
            basis, coarse_rounded, (((0,), (0,)), ((), ())), preferred_element_type=jnp.float32
        )
        weighted = (scale_column * solved).astype(jnp.bfloat16)
        spread = (
            jnp.zeros((3 * own_count, weighted.shape[1]), jnp.bfloat16).at[source_row].set(weighted)
        )
        from_next = shifted(spread[:own_count], "sub", -1)
        from_previous = shifted(spread[2 * own_count :], "sub", 1)
        return (
            spread[own_count : 2 * own_count].astype(jnp.float32)
            + from_next.astype(jnp.float32)
            + from_previous.astype(jnp.float32)
        )

    first_apply = precondition(resid)
    second_apply = precondition(first_apply)
    return (first_apply, second_apply)


def solution(mesh):
    return jax.shard_map(
        shards,
        mesh=mesh,
        in_specs=(
            P(("sub", "grp"), None),
            P(("sub", "grp"), None),
            P(("sub", "grp"), None),
            P(("sub", "grp")),
            P(("sub", "grp"), None),
            P(("sub", "grp")),
            P(("sub", "grp")),
        ),
        out_specs=(P(("sub", "grp"), None), P(("sub", "grp"), None)),
        check_vma=False,
    )
```

profile of v0, /device:TPU:7, one launch (start us, length us, event | category | flops | bytes accessed | tf_op | source)
XLA Modules:
  0.0 236.6 jit_solution(8052517843796168222)
XLA Ops:
  0.6 0.0 copy-start
  0.6 1.3 convert_element_type.56
  2.0 2.2 collective-permute-start.1
  4.1 4.0 %collective-permute-start = (bf16[1024,256]{1,0:T(8,128)(2,1)S(1)}, bf16[1024,256]{1,0:T(8,128)(2,1)S(1)}, u32[]{:S(2)}, u32[]{:S(2)}) collective-permute-start(bf16[1024,256]{1,0:T(8,128)(2,1)S(1)} %convert_element_type.56), channel_id=1, source_target_pairs={{0,4},{4,8},{8,12},{12,16},{16,20},{20,24},{24,28},{1,5},{5,9},{9,... | collective-permute-start | bytes 1572872 | tf_op jit(solution)/shard_map/ppermute | solution.py:15
  8.2 0.7 compare_select_fusion.1
  8.8 0.7 broadcast_clamp_fusion
  9.5 8.1 %collective-permute-done.1 = bf16[1024,256]{1,0:T(8,128)(2,1)S(1)} collective-permute-done((bf16[1024,256]{1,0:T(8,128)(2,1)S(1)}, bf16[1024,256]{1,0:T(8,128)(2,1)S(1)}, u32[]{:S(2)}, u32[]{:S(2)}) %collective-permute-start.1) | collective-permute-done | bytes 524320 | tf_op jit(solution)/shard_map/ppermute | solution.py:17
  17.6 12.2 %collective-permute-done = bf16[1024,256]{1,0:T(8,128)(2,1)S(1)} collective-permute-done((bf16[1024,256]{1,0:T(8,128)(2,1)S(1)}, bf16[1024,256]{1,0:T(8,128)(2,1)S(1)}, u32[]{:S(2)}, u32[]{:S(2)}) %collective-permute-start) | collective-permute-done | bytes 524320 | tf_op jit(solution)/shard_map/ppermute | solution.py:15
  29.8 0.1 pad_maximum_fusion
  29.9 0.0 copy-start.1
  29.9 7.5 %gather_fusion = bf16[2048,256]{1,0:T(8,128)(2,1)S(1)} fusion(bf16[3072,256]{1,0:T(8,128)(2,1)S(1)} %pad_maximum_fusion, s32[2048]{0:T(1024)S(1)} %get-tuple-element.8), kind=kCustom, calls=%fused_computation | custom fusion | bytes 2105344 | tf_op jit(solution)/shard_map/gather | solution.py:40
  37.5 0.0 copy-done.1
  37.5 0.3 multiply_convert_fusion.1
  37.8 0.6 gather_fusion.1
  38.4 33.2 %all-gather = bf16[512,256]{1,0:T(8,128)(2,1)S(1)} all-gather(bf16[16,256]{1,0:T(8,128)(2,1)S(1)} %gather_fusion.1), channel_id=2, replica_groups=mesh['sub'=8,'grp'=4] {'sub','grp'}, dimensions={0}, use_global_device_ids=true | all-gather | bytes 270336 | tf_op jit(solution)/shard_map/all_gather | solution.py:43
  71.6 0.0 copy-start.2
  71.6 5.8 %fusion.13 = f32[256,2048]{1,0:T(8,128)S(1)} fusion(bf16[2048,256]{1,0:T(8,128)(2,1)S(1)} %multiply_convert_fusion.1, bf16[2048,2048]{1,0:T(8,128)(2,1)} %param.8), kind=kOutput, calls=%fused_computation.33 | convolution fusion | flops 2147483648 | bytes 11534336 | tf_op jit(solution)/shard_map/dot_general | solution.py:45
  77.4 0.0 copy-done
  77.4 0.0 copy-done.2
  77.4 0.7 fusion.5
  78.2 0.5 copy.9
  78.7 9.8 %scatter_custom_fusion = bf16[3072,256]{1,0:T(8,128)(2,1)S(1)} fusion(s32[2048]{0:T(1024)S(1)} %get-tuple-element.9, bf16[2048,256]{1,0:T(8,128)(2,1)S(1)} %copy.9, bf16[]{:T(256)} %constant.4.clone.1), kind=kCustom, calls=%fused_computation.24 | custom fusion | bytes 1572866 | tf_op jit(solution)/shard_map/scatter | solution.py:51
  88.5 0.1 fusion.12
  88.6 5.8 %collective-permute-start.2 = (bf16[1024,256]{1,0:T(8,128)(2,1)S(1)}, bf16[1024,256]{1,0:T(8,128)(2,1)S(1)}, u32[]{:S(2)}, u32[]{:S(2)}) collective-permute-start(bf16[1024,256]{1,0:T(8,128)(2,1)S(1)} %get-tuple-element.6), channel_id=1, source_target_pairs={{4,0},{8,4},{12,8},{16,12},{20,16},{24,20},{28,24},{5,1},{9,5},{13... | collective-permute-start | bytes 1572872 | tf_op jit(solution)/shard_map/ppermute | solution.py:27
  94.3 1.9 collective-permute-start.3
  96.3 9.2 %collective-permute-done.2 = bf16[1024,256]{1,0:T(8,128)(2,1)S(1)} collective-permute-done((bf16[1024,256]{1,0:T(8,128)(2,1)S(1)}, bf16[1024,256]{1,0:T(8,128)(2,1)S(1)}, u32[]{:S(2)}, u32[]{:S(2)}) %collective-permute-start.2) | collective-permute-done | bytes 524320 | tf_op jit(solution)/shard_map/ppermute | solution.py:27
  105.5 10.9 %collective-permute-done.3 = bf16[1024,256]{1,0:T(8,128)(2,1)S(1)} collective-permute-done((bf16[1024,256]{1,0:T(8,128)(2,1)S(1)}, bf16[1024,256]{1,0:T(8,128)(2,1)S(1)}, u32[]{:S(2)}, u32[]{:S(2)}) %collective-permute-start.3) | collective-permute-done | bytes 524320 | tf_op jit(solution)/shard_map/ppermute | solution.py:27
  116.4 1.2 fusion.10
  117.6 1.9 collective-permute-start.5
  119.5 4.3 %collective-permute-start.4 = (bf16[1024,256]{1,0:T(8,128)(2,1)S(1)}, bf16[1024,256]{1,0:T(8,128)(2,1)S(1)}, u32[]{:S(2)}, u32[]{:S(2)}) collective-permute-start(bf16[1024,256]{1,0:T(8,128)(2,1)S(1)} %get-tuple-element.2), channel_id=1, source_target_pairs={{0,4},{4,8},{8,12},{12,16},{16,20},{20,24},{24,28},{1,5},{5,9},{9,... | collective-permute-start | bytes 1572872 | tf_op jit(solution)/shard_map/ppermute | solution.py:15
  123.8 9.7 %collective-permute-done.5 = bf16[1024,256]{1,0:T(8,128)(2,1)S(1)} collective-permute-done((bf16[1024,256]{1,0:T(8,128)(2,1)S(1)}, bf16[1024,256]{1,0:T(8,128)(2,1)S(1)}, u32[]{:S(2)}, u32[]{:S(2)}) %collective-permute-start.5) | collective-permute-done | bytes 524320 | tf_op jit(solution)/shard_map/ppermute | solution.py:17
  133.4 12.0 %collective-permute-done.4 = bf16[1024,256]{1,0:T(8,128)(2,1)S(1)} collective-permute-done((bf16[1024,256]{1,0:T(8,128)(2,1)S(1)}, bf16[1024,256]{1,0:T(8,128)(2,1)S(1)}, u32[]{:S(2)}, u32[]{:S(2)}) %collective-permute-start.4) | collective-permute-done | bytes 524320 | tf_op jit(solution)/shard_map/ppermute | solution.py:15
  145.5 0.1 pad_maximum_fusion.1
  145.6 7.5 %gather_fusion.2 = bf16[2048,256]{1,0:T(8,128)(2,1)S(1)} fusion(bf16[3072,256]{1,0:T(8,128)(2,1)S(1)} %pad_maximum_fusion.1, s32[2048]{0:T(1024)S(1)} %get-tuple-element.8), kind=kCustom, calls=%fused_computation.2 | custom fusion | bytes 2105344 | tf_op jit(solution)/shard_map/gather | solution.py:40
  153.1 0.3 multiply_convert_fusion
  153.4 0.6 gather_fusion.3
  154.0 5.8 %fusion.14 = f32[256,2048]{1,0:T(8,128)S(1)} fusion(bf16[2048,256]{1,0:T(8,128)(2,1)S(1)} %multiply_convert_fusion, bf16[2048,2048]{1,0:T(8,128)(2,1)} %param.8), kind=kOutput, calls=%fused_computation.34 | convolution fusion | flops 2147483648 | bytes 11534336 | tf_op jit(solution)/shard_map/dot_general | solution.py:45
  159.8 36.6 %all-gather.1 = bf16[512,256]{1,0:T(8,128)(2,1)S(1)} all-gather(bf16[16,256]{1,0:T(8,128)(2,1)S(1)} %gather_fusion.3), channel_id=3, replica_groups=mesh['sub'=8,'grp'=4] {'sub','grp'}, dimensions={0}, use_global_device_ids=true | all-gather | bytes 270336 | tf_op jit(solution)/shard_map/all_gather | solution.py:43
  196.4 0.7 fusion.4
  197.1 0.5 copy.10
  197.7 9.8 %scatter_custom_fusion.1 = bf16[3072,256]{1,0:T(8,128)(2,1)S(1)} fusion(s32[2048]{0:T(1024)S(1)} %get-tuple-element.9, bf16[2048,256]{1,0:T(8,128)(2,1)S(1)} %copy.10, bf16[]{:T(256)} %constant.4.clone.1), kind=kCustom, calls=%fused_computation.22 | custom fusion | bytes 1572866 | tf_op jit(solution)/shard_map/scatter | solution.py:51
  207.5 0.1 fusion.11
  207.5 5.8 %collective-permute-start.6 = (bf16[1024,256]{1,0:T(8,128)(2,1)S(1)}, bf16[1024,256]{1,0:T(8,128)(2,1)S(1)}, u32[]{:S(2)}, u32[]{:S(2)}) collective-permute-start(bf16[1024,256]{1,0:T(8,128)(2,1)S(1)} %get-tuple-element.4), channel_id=1, source_target_pairs={{4,0},{8,4},{12,8},{16,12},{20,16},{24,20},{28,24},{5,1},{9,5},{13... | collective-permute-start | bytes 1572872 | tf_op jit(solution)/shard_map/ppermute | solution.py:27
  213.3 1.9 collective-permute-start.7
  215.3 9.2 %collective-permute-done.6 = bf16[1024,256]{1,0:T(8,128)(2,1)S(1)} collective-permute-done((bf16[1024,256]{1,0:T(8,128)(2,1)S(1)}, bf16[1024,256]{1,0:T(8,128)(2,1)S(1)}, u32[]{:S(2)}, u32[]{:S(2)}) %collective-permute-start.6) | collective-permute-done | bytes 524320 | tf_op jit(solution)/shard_map/ppermute | solution.py:27
  224.5 10.9 %collective-permute-done.7 = bf16[1024,256]{1,0:T(8,128)(2,1)S(1)} collective-permute-done((bf16[1024,256]{1,0:T(8,128)(2,1)S(1)}, bf16[1024,256]{1,0:T(8,128)(2,1)S(1)}, u32[]{:S(2)}, u32[]{:S(2)}) %collective-permute-start.7) | collective-permute-done | bytes 524320 | tf_op jit(solution)/shard_map/ppermute | solution.py:27
  235.4 1.1 convert_add_fusion
  (1 shorter events, 0.0 us)
Async XLA Ops:
  0.6 76.8 %copy-start = (bf16[16,2048]{1,0:T(8,128)(2,1)S(1)}, bf16[16,2048]{1,0:T(8,128)(2,1)}, u32[]{:S(2)}) copy-start(bf16[16,2048]{1,0:T(8,128)(2,1)} %param.9) | copy-start | bytes 196612
  2.0 15.6 %collective-permute-start.1 = (bf16[1024,256]{1,0:T(8,128)(2,1)S(1)}, bf16[1024,256]{1,0:T(8,128)(2,1)S(1)}, u32[]{:S(2)}, u32[]{:S(2)}) collective-permute-start(bf16[1024,256]{1,0:T(8,128)(2,1)S(1)} %convert_element_type.56), channel_id=1, source_target_pairs={{4,0},{8,4},{12,8},{16,12},{20,16},{24,20},{28,24},{5,1},{9,5},{13... | collective-permute-start | bytes 1572872 | tf_op jit(solution)/shard_map/ppermute | solution.py:17
  4.1 25.7 %collective-permute-start = (bf16[1024,256]{1,0:T(8,128)(2,1)S(1)}, bf16[1024,256]{1,0:T(8,128)(2,1)S(1)}, u32[]{:S(2)}, u32[]{:S(2)}) collective-permute-start(bf16[1024,256]{1,0:T(8,128)(2,1)S(1)} %convert_element_type.56), channel_id=1, source_target_pairs={{0,4},{4,8},{8,12},{12,16},{16,20},{20,24},{24,28},{1,5},{5,9},{9,... | collective-permute-start | bytes 1572872 | tf_op jit(solution)/shard_map/ppermute | solution.py:15
  29.9 7.5 %copy-start.1 = (f32[2048]{0:T(1024)S(1)}, f32[2048]{0:T(1024)}, u32[]{:S(2)}) copy-start(f32[2048]{0:T(1024)} %param.10) | copy-start | bytes 24580
  71.6 5.8 %copy-start.2 = (bf16[16,512]{1,0:T(8,128)(2,1)S(1)}, bf16[16,512]{1,0:T(8,128)(2,1)}, u32[]{:S(2)}) copy-start(bf16[16,512]{1,0:T(8,128)(2,1)} %param.11) | copy-start | bytes 49156
  88.6 16.9 %collective-permute-start.2 = (bf16[1024,256]{1,0:T(8,128)(2,1)S(1)}, bf16[1024,256]{1,0:T(8,128)(2,1)S(1)}, u32[]{:S(2)}, u32[]{:S(2)}) collective-permute-start(bf16[1024,256]{1,0:T(8,128)(2,1)S(1)} %get-tuple-element.6), channel_id=1, source_target_pairs={{4,0},{8,4},{12,8},{16,12},{20,16},{24,20},{28,24},{5,1},{9,5},{13... | collective-permute-start | bytes 1572872 | tf_op jit(solution)/shard_map/ppermute | solution.py:27
  94.3 22.1 %collective-permute-start.3 = (bf16[1024,256]{1,0:T(8,128)(2,1)S(1)}, bf16[1024,256]{1,0:T(8,128)(2,1)S(1)}, u32[]{:S(2)}, u32[]{:S(2)}) collective-permute-start(bf16[1024,256]{1,0:T(8,128)(2,1)S(1)} %get-tuple-element.7), channel_id=1, source_target_pairs={{0,4},{4,8},{8,12},{12,16},{16,20},{20,24},{24,28},{1,5},{5,9},{9,... | collective-permute-start | bytes 1572872 | tf_op jit(solution)/shard_map/ppermute | solution.py:27
  117.6 15.8 %collective-permute-start.5 = (bf16[1024,256]{1,0:T(8,128)(2,1)S(1)}, bf16[1024,256]{1,0:T(8,128)(2,1)S(1)}, u32[]{:S(2)}, u32[]{:S(2)}) collective-permute-start(bf16[1024,256]{1,0:T(8,128)(2,1)S(1)} %get-tuple-element.2), channel_id=1, source_target_pairs={{4,0},{8,4},{12,8},{16,12},{20,16},{24,20},{28,24},{5,1},{9,5},{13... | collective-permute-start | bytes 1572872 | tf_op jit(solution)/shard_map/ppermute | solution.py:17
  119.5 25.9 %collective-permute-start.4 = (bf16[1024,256]{1,0:T(8,128)(2,1)S(1)}, bf16[1024,256]{1,0:T(8,128)(2,1)S(1)}, u32[]{:S(2)}, u32[]{:S(2)}) collective-permute-start(bf16[1024,256]{1,0:T(8,128)(2,1)S(1)} %get-tuple-element.2), channel_id=1, source_target_pairs={{0,4},{4,8},{8,12},{12,16},{16,20},{20,24},{24,28},{1,5},{5,9},{9,... | collective-permute-start | bytes 1572872 | tf_op jit(solution)/shard_map/ppermute | solution.py:15
  207.5 16.9 %collective-permute-start.6 = (bf16[1024,256]{1,0:T(8,128)(2,1)S(1)}, bf16[1024,256]{1,0:T(8,128)(2,1)S(1)}, u32[]{:S(2)}, u32[]{:S(2)}) collective-permute-start(bf16[1024,256]{1,0:T(8,128)(2,1)S(1)} %get-tuple-element.4), channel_id=1, source_target_pairs={{4,0},{8,4},{12,8},{16,12},{20,16},{24,20},{28,24},{5,1},{9,5},{13... | collective-permute-start | bytes 1572872 | tf_op jit(solution)/shard_map/ppermute | solution.py:27
  213.3 22.1 %collective-permute-start.7 = (bf16[1024,256]{1,0:T(8,128)(2,1)S(1)}, bf16[1024,256]{1,0:T(8,128)(2,1)S(1)}, u32[]{:S(2)}, u32[]{:S(2)}) collective-permute-start(bf16[1024,256]{1,0:T(8,128)(2,1)S(1)} %get-tuple-element.5), channel_id=1, source_target_pairs={{0,4},{4,8},{8,12},{12,16},{16,20},{20,24},{24,28},{1,5},{5,9},{9,... | collective-permute-start | bytes 1572872 | tf_op jit(solution)/shard_map/ppermute | solution.py:27
where the time goes:
time: 237 us
  waiting for transfers between devices  82.3 us (35%)
  blocking collectives  69.9 us (29%)
  local copies, waits for them, and re-layouts  36.9 us (16%)
  starting transfers between devices  27.8 us (12%)
  matrix products  13 us (5%)
  other arithmetic  5.86 us (2%)
    all_gather x2, blocking collectives, precondition(): coarse = add_all(lax.all_gather(primal, ('sub', 'grp'), axis=0, tiled=True))  69.9 us
    ppermute x4, waiting for transfers between devices, shifted(): return lax.ppermute(shard, axis, pairs)  40.3 us
    ppermute x2, waiting for transfers between devices, with_halo(): lax.ppermute(tail, axis, [(i, (i + 1) % count) for i in range(ends)])  24.3 us
    scatter x2, local copies, waits for them, and re-layouts, precondition(): jnp.zeros((3 * own_count, weighted.shape[1]), jnp.bfloat16).at[source_row]  19.6 us
    ppermute x2, waiting for transfers between devices, with_halo(): lax.ppermute(head, axis, [((i + 1) % count, i) for i in range(ends)])  17.7 us
    ppermute x4, starting transfers between devices, shifted(): return lax.ppermute(shard, axis, pairs)  15.4 us
    gather x2, local copies, waits for them, and re-layouts, precondition(): gathered = padded[source_row]  15 us
    dot_general x2, matrix products, precondition(): solved = jnp.dot(schur_inv, scaled, preferred_element_type=jnp.float32)  11.5 us
  transfers between devices with their start and end apart: 8, of which 8 were waited for; matrix products, arithmetic and copies ran while one was open for 1% of the time, Pallas kernels for 0%

commit v1 on v0

--- a/solution.py
+++ b/solution.py
@@ -2,6 +2,20 @@
 import jax.numpy as jnp
 from jax import lax
 from jax.sharding import PartitionSpec as P
+
+
+def put_chains(target):
+    group_axis = ("sub", "grp")
+    f_now = lax.axis_size(group_axis)
+    local_next, raw_out, side_arr = (f_now, lax.axis_index(group_axis), target.shape[0])
+    local_now, y = (target, 1)
+    while y < local_next:
+        heap = []
+        for src_i in range(local_next):
+            heap.append((src_i, (src_i - y) % local_next))
+        local_now = jnp.concatenate([local_now, lax.ppermute(local_now, group_axis, heap)], 0)
+        y = 2 * y
+    return jnp.roll(local_now, raw_out * side_arr, 0)
 
 
 def with_halo(cells, sides, width):
@@ -40,7 +54,7 @@
         gathered = padded[source_row]
         scaled = (scale_column * gathered.astype(jnp.float32)).astype(jnp.bfloat16)
         primal = scaled[primal_idx]
-        coarse = add_all(lax.all_gather(primal, ("sub", "grp"), axis=0, tiled=True))
+        coarse = add_all(put_chains(primal))
         coarse_rounded = coarse.astype(jnp.bfloat16)
         solved = jnp.dot(schur_inv, scaled, preferred_element_type=jnp.float32)
         solved = solved + lax.dot_general(

time: 237 us -> 210 us (0.89)
  blocking collectives: 69.9 us -> 0 us
  waiting for transfers between devices: 82.3 us -> 120 us
  starting transfers between devices: 27.8 us -> 32 us
    all_gather x2 -> x0, blocking collectives: 69.9 us -> none  [precondition(): coarse = add_all(lax.all_gather(primal, ('sub', 'grp'), axis=0, tiled=True))]
    ppermute x0 -> x10, waiting for transfers between devices: none -> 34.6 us  [put_chains(): lax.ppermute(local_now, group_axis, heap)]
    ppermute x0 -> x10, starting transfers between devices: none -> 7.32 us  [put_chains(): lax.ppermute(local_now, group_axis, heap)]
    ppermute x4, starting transfers between devices: 15.4 us -> 12.4 us  [shifted(): return lax.ppermute(shard, axis, pairs)]
    ppermute x4, waiting for transfers between devices: 40.3 us -> 43.4 us  [shifted(): return lax.ppermute(shard, axis, pairs)]
  transfers between devices with their start and end apart: 8 -> 18, of which waited for: 8 -> 18; matrix products, arithmetic and copies ran while one was open for 1% -> 6% of each run, Pallas kernels for 0% -> 0%
where the time goes in v1:
time: 210 us
  waiting for transfers between devices  120 us (57%)
  local copies, waits for them, and re-layouts  37 us (18%)
  starting transfers between devices  32 us (15%)
  matrix products  13.8 us (7%)
  other arithmetic  5.88 us (3%)
    ppermute x4, waiting for transfers between devices, shifted(): return lax.ppermute(shard, axis, pairs)  43.4 us
    ppermute x10, waiting for transfers between devices, put_chains(): lax.ppermute(local_now, group_axis, heap)  34.6 us
    ppermute x2, waiting for transfers between devices, with_halo(): lax.ppermute(tail, axis, [(i, (i + 1) % count) for i in range(ends)])  24.3 us
    scatter x2, local copies, waits for them, and re-layouts, precondition(): jnp.zeros((3 * own_count, weighted.shape[1]), jnp.bfloat16).at[source_row]  19.6 us
    ppermute x2, waiting for transfers between devices, with_halo(): lax.ppermute(head, axis, [((i + 1) % count, i) for i in range(ends)])  17.7 us
    gather x2, local copies, waits for them, and re-layouts, precondition(): gathered = padded[source_row]  15 us
    ppermute x4, starting transfers between devices, shifted(): return lax.ppermute(shard, axis, pairs)  12.4 us
    dot_general x2, matrix products, precondition(): solved = jnp.dot(schur_inv, scaled, preferred_element_type=jnp.float32)  11.5 us
  transfers between devices with their start and end apart: 18, of which 18 were waited for; matrix products, arithmetic and copies ran while one was open for 6% of the time, Pallas kernels for 0%

profile of v1, /device:TPU:7, one launch (start us, length us, event | category | flops | bytes accessed | tf_op | source)
XLA Modules:
  0.0 209.6 jit_solution(1834717620619819092)
XLA Ops:
  0.6 0.0 copy-start
  0.6 1.3 convert_element_type.56
  2.0 2.2 %collective-permute-start.1 = (bf16[1024,256]{1,0:T(8,128)(2,1)S(1)}, bf16[1024,256]{1,0:T(8,128)(2,1)S(1)}, u32[]{:S(2)}, u32[]{:S(2)}) collective-permute-start(bf16[1024,256]{1,0:T(8,128)(2,1)S(1)} %convert_element_type.56), channel_id=1, source_target_pairs={{4,0},{8,4},{12,8},{16,12},{20,16},{24,20},{28,24},{5,1},{9,5},{13... | collective-permute-start | bytes 1572872 | tf_op jit(solution)/shard_map/ppermute | solution.py:31
  4.1 4.0 %collective-permute-start = (bf16[1024,256]{1,0:T(8,128)(2,1)S(1)}, bf16[1024,256]{1,0:T(8,128)(2,1)S(1)}, u32[]{:S(2)}, u32[]{:S(2)}) collective-permute-start(bf16[1024,256]{1,0:T(8,128)(2,1)S(1)} %convert_element_type.56), channel_id=1, source_target_pairs={{0,4},{4,8},{8,12},{12,16},{16,20},{20,24},{24,28},{1,5},{5,9},{9,... | collective-permute-start | bytes 1572872 | tf_op jit(solution)/shard_map/ppermute | solution.py:29
  8.2 0.7 compare_select_fusion.1
  8.8 0.7 broadcast_clamp_fusion
  9.5 8.0 %collective-permute-done.1 = bf16[1024,256]{1,0:T(8,128)(2,1)S(1)} collective-permute-done((bf16[1024,256]{1,0:T(8,128)(2,1)S(1)}, bf16[1024,256]{1,0:T(8,128)(2,1)S(1)}, u32[]{:S(2)}, u32[]{:S(2)}) %collective-permute-start.1) | collective-permute-done | bytes 524320 | tf_op jit(solution)/shard_map/ppermute | solution.py:31
  17.6 12.2 %collective-permute-done = bf16[1024,256]{1,0:T(8,128)(2,1)S(1)} collective-permute-done((bf16[1024,256]{1,0:T(8,128)(2,1)S(1)}, bf16[1024,256]{1,0:T(8,128)(2,1)S(1)}, u32[]{:S(2)}, u32[]{:S(2)}) %collective-permute-start) | collective-permute-done | bytes 524320 | tf_op jit(solution)/shard_map/ppermute | solution.py:29
  29.8 0.1 pad_maximum_fusion
  29.9 0.0 copy-start.1
  29.9 7.5 %gather_fusion = bf16[2048,256]{1,0:T(8,128)(2,1)S(1)} fusion(bf16[3072,256]{1,0:T(8,128)(2,1)S(1)} %pad_maximum_fusion, s32[2048]{0:T(1024)S(1)} %get-tuple-element.29), kind=kCustom, calls=%fused_computation | custom fusion | bytes 2105344 | tf_op jit(solution)/shard_map/gather | solution.py:54
  37.5 0.0 copy-done.1
  37.5 0.3 multiply_convert_fusion.1
  37.8 0.6 gather_fusion.1
  38.4 0.5 collective-permute-start.2
  39.0 4.4 %collective-permute-done.2 = bf16[16,256]{1,0:T(8,128)(2,1)S(1)} collective-permute-done((bf16[16,256]{1,0:T(8,128)(2,1)S(1)}, bf16[16,256]{1,0:T(8,128)(2,1)S(1)}, u32[]{:S(2)}, u32[]{:S(2)}) %collective-permute-start.2) | collective-permute-done | bytes 8224 | tf_op jit(solution)/shard_map/ppermute | solution.py:16
  43.3 0.0 collective-permute-start.3
  43.3 4.4 %collective-permute-done.3 = bf16[32,256]{1,0:T(8,128)(2,1)S(1)} collective-permute-done((bf16[32,256]{1,0:T(8,128)(2,1)S(1)}, bf16[32,256]{1,0:T(8,128)(2,1)S(1)}, u32[]{:S(2)}, u32[]{:S(2)}) %collective-permute-start.3) | collective-permute-done | bytes 16416 | tf_op jit(solution)/shard_map/ppermute | solution.py:16
  47.7 0.0 collective-permute-start.4
  47.7 3.7 %collective-permute-done.4 = bf16[64,256]{1,0:T(8,128)(2,1)S(1)} collective-permute-done((bf16[64,256]{1,0:T(8,128)(2,1)S(1)}, bf16[64,256]{1,0:T(8,128)(2,1)S(1)}, u32[]{:S(2)}, u32[]{:S(2)}) %collective-permute-start.4) | collective-permute-done | bytes 32800 | tf_op jit(solution)/shard_map/ppermute | solution.py:16
  51.4 4.8 %collective-permute-start.5 = (bf16[128,256]{1,0:T(8,128)(2,1)S(1)}, bf16[128,256]{1,0:T(8,128)(2,1)S(1)}, u32[]{:S(2)}, u32[]{:S(2)}) collective-permute-start(bf16[128,256]{1,0:T(8,128)(2,1)S(1)} %pad_maximum_fusion.2), channel_id=1, source_target_pairs={{0,24},{1,25},{2,26},{3,27},{4,28},{5,29},{6,30},{7,31},{8,0},{9,1... | collective-permute-start | bytes 196616 | tf_op jit(solution)/shard_map/ppermute | solution.py:16
  56.2 1.3 collective-permute-done.5
  57.6 0.0 copy-start.2
  57.6 0.7 collective-permute-start.6
  58.2 5.8 %fusion.27 = f32[256,2048]{1,0:T(8,128)S(1)} fusion(bf16[2048,256]{1,0:T(8,128)(2,1)S(1)} %multiply_convert_fusion.1, bf16[2048,2048]{1,0:T(8,128)(2,1)} %param.10), kind=kOutput, calls=%fused_computation.71 | convolution fusion | flops 2147483648 | bytes 11534336 | tf_op jit(solution)/shard_map/dot_general | solution.py:59
  64.0 2.6 %collective-permute-done.6 = bf16[256,256]{1,0:T(8,128)(2,1)S(1)} collective-permute-done((bf16[256,256]{1,0:T(8,128)(2,1)S(1)}, bf16[256,256]{1,0:T(8,128)(2,1)S(1)}, u32[]{:S(2)}, u32[]{:S(2)}) %collective-permute-start.6) | collective-permute-done | bytes 131104 | tf_op jit(solution)/shard_map/ppermute | solution.py:16
  66.6 0.0 copy-done
  66.6 1.1 fusion.5
  67.8 0.5 copy.9
  68.3 9.8 %scatter_custom_fusion = bf16[3072,256]{1,0:T(8,128)(2,1)S(1)} fusion(s32[2048]{0:T(1024)S(1)} %get-tuple-element.30, bf16[2048,256]{1,0:T(8,128)(2,1)S(1)} %copy.9, bf16[]{:T(256)} %constant.30.clone.1), kind=kCustom, calls=%fused_computation.24 | custom fusion | bytes 1572866 | tf_op jit(solution)/shard_map/scatter | solution.py:65
  78.1 0.1 fusion.26
  78.2 1.9 collective-permute-start.7
  80.1 4.3 %collective-permute-start.8 = (bf16[1024,256]{1,0:T(8,128)(2,1)S(1)}, bf16[1024,256]{1,0:T(8,128)(2,1)S(1)}, u32[]{:S(2)}, u32[]{:S(2)}) collective-permute-start(bf16[1024,256]{1,0:T(8,128)(2,1)S(1)} %get-tuple-element.8), channel_id=1, source_target_pairs={{0,4},{4,8},{8,12},{12,16},{16,20},{20,24},{24,28},{1,5},{5,9},{9,... | collective-permute-start | bytes 1572872 | tf_op jit(solution)/shard_map/ppermute | solution.py:41
  84.4 9.7 %collective-permute-done.7 = bf16[1024,256]{1,0:T(8,128)(2,1)S(1)} collective-permute-done((bf16[1024,256]{1,0:T(8,128)(2,1)S(1)}, bf16[1024,256]{1,0:T(8,128)(2,1)S(1)}, u32[]{:S(2)}, u32[]{:S(2)}) %collective-permute-start.7) | collective-permute-done | bytes 524320 | tf_op jit(solution)/shard_map/ppermute | solution.py:41
  94.1 11.9 %collective-permute-done.8 = bf16[1024,256]{1,0:T(8,128)(2,1)S(1)} collective-permute-done((bf16[1024,256]{1,0:T(8,128)(2,1)S(1)}, bf16[1024,256]{1,0:T(8,128)(2,1)S(1)}, u32[]{:S(2)}, u32[]{:S(2)}) %collective-permute-start.8) | collective-permute-done | bytes 524320 | tf_op jit(solution)/shard_map/ppermute | solution.py:41
  106.0 1.2 fusion.24
  107.2 1.9 collective-permute-start.10
  109.1 4.3 %collective-permute-start.9 = (bf16[1024,256]{1,0:T(8,128)(2,1)S(1)}, bf16[1024,256]{1,0:T(8,128)(2,1)S(1)}, u32[]{:S(2)}, u32[]{:S(2)}) collective-permute-start(bf16[1024,256]{1,0:T(8,128)(2,1)S(1)} %get-tuple-element.3), channel_id=1, source_target_pairs={{0,4},{4,8},{8,12},{12,16},{16,20},{20,24},{24,28},{1,5},{5,9},{9,... | collective-permute-start | bytes 1572872 | tf_op jit(solution)/shard_map/ppermute | solution.py:29
  113.4 9.7 %collective-permute-done.10 = bf16[1024,256]{1,0:T(8,128)(2,1)S(1)} collective-permute-done((bf16[1024,256]{1,0:T(8,128)(2,1)S(1)}, bf16[1024,256]{1,0:T(8,128)(2,1)S(1)}, u32[]{:S(2)}, u32[]{:S(2)}) %collective-permute-start.10) | collective-permute-done | bytes 524320 | tf_op jit(solution)/shard_map/ppermute | solution.py:31
  123.0 12.0 %collective-permute-done.9 = bf16[1024,256]{1,0:T(8,128)(2,1)S(1)} collective-permute-done((bf16[1024,256]{1,0:T(8,128)(2,1)S(1)}, bf16[1024,256]{1,0:T(8,128)(2,1)S(1)}, u32[]{:S(2)}, u32[]{:S(2)}) %collective-permute-start.9) | collective-permute-done | bytes 524320 | tf_op jit(solution)/shard_map/ppermute | solution.py:29
  135.1 0.1 pad_maximum_fusion.1
  135.2 7.5 %gather_fusion.2 = bf16[2048,256]{1,0:T(8,128)(2,1)S(1)} fusion(bf16[3072,256]{1,0:T(8,128)(2,1)S(1)} %pad_maximum_fusion.1, s32[2048]{0:T(1024)S(1)} %get-tuple-element.29), kind=kCustom, calls=%fused_computation.2 | custom fusion | bytes 2105344 | tf_op jit(solution)/shard_map/gather | solution.py:54
  142.7 0.3 multiply_convert_fusion
  143.0 0.6 gather_fusion.3
  143.6 0.5 collective-permute-start.11
  144.2 4.4 %collective-permute-done.11 = bf16[16,256]{1,0:T(8,128)(2,1)S(1)} collective-permute-done((bf16[16,256]{1,0:T(8,128)(2,1)S(1)}, bf16[16,256]{1,0:T(8,128)(2,1)S(1)}, u32[]{:S(2)}, u32[]{:S(2)}) %collective-permute-start.11) | collective-permute-done | bytes 8224 | tf_op jit(solution)/shard_map/ppermute | solution.py:16
  148.6 0.0 collective-permute-start.12
  148.6 4.4 %collective-permute-done.12 = bf16[32,256]{1,0:T(8,128)(2,1)S(1)} collective-permute-done((bf16[32,256]{1,0:T(8,128)(2,1)S(1)}, bf16[32,256]{1,0:T(8,128)(2,1)S(1)}, u32[]{:S(2)}, u32[]{:S(2)}) %collective-permute-start.12) | collective-permute-done | bytes 16416 | tf_op jit(solution)/shard_map/ppermute | solution.py:16
  152.9 0.0 collective-permute-start.13
  153.0 3.7 %collective-permute-done.13 = bf16[64,256]{1,0:T(8,128)(2,1)S(1)} collective-permute-done((bf16[64,256]{1,0:T(8,128)(2,1)S(1)}, bf16[64,256]{1,0:T(8,128)(2,1)S(1)}, u32[]{:S(2)}, u32[]{:S(2)}) %collective-permute-start.13) | collective-permute-done | bytes 32800 | tf_op jit(solution)/shard_map/ppermute | solution.py:16
  156.6 0.7 collective-permute-start.14
  157.3 2.9 %collective-permute-done.14 = bf16[128,256]{1,0:T(8,128)(2,1)S(1)} collective-permute-done((bf16[128,256]{1,0:T(8,128)(2,1)S(1)}, bf16[128,256]{1,0:T(8,128)(2,1)S(1)}, u32[]{:S(2)}, u32[]{:S(2)}) %collective-permute-start.14) | collective-permute-done | bytes 65568 | tf_op jit(solution)/shard_map/ppermute | solution.py:16
  160.2 0.1 collective-permute-start.15
  160.3 5.8 %fusion.28 = f32[256,2048]{1,0:T(8,128)S(1)} fusion(bf16[2048,256]{1,0:T(8,128)(2,1)S(1)} %multiply_convert_fusion, bf16[2048,2048]{1,0:T(8,128)(2,1)} %param.10), kind=kOutput, calls=%fused_computation.72 | convolution fusion | flops 2147483648 | bytes 11534336 | tf_op jit(solution)/shard_map/dot_general | solution.py:59
  166.1 2.9 %collective-permute-done.15 = bf16[256,256]{1,0:T(8,128)(2,1)S(1)} collective-permute-done((bf16[256,256]{1,0:T(8,128)(2,1)S(1)}, bf16[256,256]{1,0:T(8,128)(2,1)S(1)}, u32[]{:S(2)}, u32[]{:S(2)}) %collective-permute-start.15) | collective-permute-done | bytes 131104 | tf_op jit(solution)/shard_map/ppermute | solution.py:16
  169.0 1.1 fusion.4
  170.2 0.5 copy.10
  170.7 9.8 %scatter_custom_fusion.1 = bf16[3072,256]{1,0:T(8,128)(2,1)S(1)} fusion(s32[2048]{0:T(1024)S(1)} %get-tuple-element.30, bf16[2048,256]{1,0:T(8,128)(2,1)S(1)} %copy.10, bf16[]{:T(256)} %constant.30.clone.1), kind=kCustom, calls=%fused_computation.22 | custom fusion | bytes 1572866 | tf_op jit(solution)/shard_map/scatter | solution.py:65
  180.5 0.1 fusion.25
  180.6 1.9 collective-permute-start.16
  182.5 4.3 %collective-permute-start.17 = (bf16[1024,256]{1,0:T(8,128)(2,1)S(1)}, bf16[1024,256]{1,0:T(8,128)(2,1)S(1)}, u32[]{:S(2)}, u32[]{:S(2)}) collective-permute-start(bf16[1024,256]{1,0:T(8,128)(2,1)S(1)} %get-tuple-element.6), channel_id=1, source_target_pairs={{0,4},{4,8},{8,12},{12,16},{16,20},{20,24},{24,28},{1,5},{5,9},{9,... | collective-permute-start | bytes 1572872 | tf_op jit(solution)/shard_map/ppermute | solution.py:41
  186.8 9.2 %collective-permute-done.16 = bf16[1024,256]{1,0:T(8,128)(2,1)S(1)} collective-permute-done((bf16[1024,256]{1,0:T(8,128)(2,1)S(1)}, bf16[1024,256]{1,0:T(8,128)(2,1)S(1)}, u32[]{:S(2)}, u32[]{:S(2)}) %collective-permute-start.16) | collective-permute-done | bytes 524320 | tf_op jit(solution)/shard_map/ppermute | solution.py:41
  195.9 12.5 %collective-permute-done.17 = bf16[1024,256]{1,0:T(8,128)(2,1)S(1)} collective-permute-done((bf16[1024,256]{1,0:T(8,128)(2,1)S(1)}, bf16[1024,256]{1,0:T(8,128)(2,1)S(1)}, u32[]{:S(2)}, u32[]{:S(2)}) %collective-permute-start.17) | collective-permute-done | bytes 524320 | tf_op jit(solution)/shard_map/ppermute | solution.py:41
  208.5 1.1 convert_add_fusion
  (20 shorter events, 0.1 us)
Async XLA Ops:
  0.6 66.0 %copy-start = (bf16[16,2048]{1,0:T(8,128)(2,1)S(1)}, bf16[16,2048]{1,0:T(8,128)(2,1)}, u32[]{:S(2)}) copy-start(bf16[16,2048]{1,0:T(8,128)(2,1)} %param.11) | copy-start | bytes 196612
  2.0 15.6 %collective-permute-start.1 = (bf16[1024,256]{1,0:T(8,128)(2,1)S(1)}, bf16[1024,256]{1,0:T(8,128)(2,1)S(1)}, u32[]{:S(2)}, u32[]{:S(2)}) collective-permute-start(bf16[1024,256]{1,0:T(8,128)(2,1)S(1)} %convert_element_type.56), channel_id=1, source_target_pairs={{4,0},{8,4},{12,8},{16,12},{20,16},{24,20},{28,24},{5,1},{9,5},{13... | collective-permute-start | bytes 1572872 | tf_op jit(solution)/shard_map/ppermute | solution.py:31
  4.1 25.7 %collective-permute-start = (bf16[1024,256]{1,0:T(8,128)(2,1)S(1)}, bf16[1024,256]{1,0:T(8,128)(2,1)S(1)}, u32[]{:S(2)}, u32[]{:S(2)}) collective-permute-start(bf16[1024,256]{1,0:T(8,128)(2,1)S(1)} %convert_element_type.56), channel_id=1, source_target_pairs={{0,4},{4,8},{8,12},{12,16},{16,20},{20,24},{24,28},{1,5},{5,9},{9,... | collective-permute-start | bytes 1572872 | tf_op jit(solution)/shard_map/ppermute | solution.py:29
  29.9 7.5 %copy-start.1 = (f32[2048]{0:T(1024)S(1)}, f32[2048]{0:T(1024)}, u32[]{:S(2)}) copy-start(f32[2048]{0:T(1024)} %param.12) | copy-start | bytes 24580
  38.4 4.9 %collective-permute-start.2 = (bf16[16,256]{1,0:T(8,128)(2,1)S(1)}, bf16[16,256]{1,0:T(8,128)(2,1)S(1)}, u32[]{:S(2)}, u32[]{:S(2)}) collective-permute-start(bf16[16,256]{1,0:T(8,128)(2,1)S(1)} %gather_fusion.1), channel_id=1, source_target_pairs={{0,31},{1,0},{2,1},{3,2},{4,3},{5,4},{6,5},{7,6},{8,7},{9,8},{10,9... | collective-permute-start | bytes 24584 | tf_op jit(solution)/shard_map/ppermute | solution.py:16
  43.3 4.4 %collective-permute-start.3 = (bf16[32,256]{1,0:T(8,128)(2,1)S(1)}, bf16[32,256]{1,0:T(8,128)(2,1)S(1)}, u32[]{:S(2)}, u32[]{:S(2)}) collective-permute-start(bf16[32,256]{1,0:T(8,128)(2,1)S(1)} %pad_maximum_fusion.6), channel_id=1, source_target_pairs={{0,30},{1,31},{2,0},{3,1},{4,2},{5,3},{6,4},{7,5},{8,6},{9,7},{10,... | collective-permute-start | bytes 49160 | tf_op jit(solution)/shard_map/ppermute | solution.py:16
  47.7 3.7 %collective-permute-start.4 = (bf16[64,256]{1,0:T(8,128)(2,1)S(1)}, bf16[64,256]{1,0:T(8,128)(2,1)S(1)}, u32[]{:S(2)}, u32[]{:S(2)}) collective-permute-start(bf16[64,256]{1,0:T(8,128)(2,1)S(1)} %pad_maximum_fusion.4), channel_id=1, source_target_pairs={{0,28},{1,29},{2,30},{3,31},{4,0},{5,1},{6,2},{7,3},{8,4},{9,5},{1... | collective-permute-start | bytes 98312 | tf_op jit(solution)/shard_map/ppermute | solution.py:16
  51.4 6.2 %collective-permute-start.5 = (bf16[128,256]{1,0:T(8,128)(2,1)S(1)}, bf16[128,256]{1,0:T(8,128)(2,1)S(1)}, u32[]{:S(2)}, u32[]{:S(2)}) collective-permute-start(bf16[128,256]{1,0:T(8,128)(2,1)S(1)} %pad_maximum_fusion.2), channel_id=1, source_target_pairs={{0,24},{1,25},{2,26},{3,27},{4,28},{5,29},{6,30},{7,31},{8,0},{9,1... | collective-permute-start | bytes 196616 | tf_op jit(solution)/shard_map/ppermute | solution.py:16
  57.6 9.0 %copy-start.2 = (bf16[16,512]{1,0:T(8,128)(2,1)S(1)}, bf16[16,512]{1,0:T(8,128)(2,1)}, u32[]{:S(2)}) copy-start(bf16[16,512]{1,0:T(8,128)(2,1)} %param.13) | copy-start | bytes 49156
  57.6 9.0 %collective-permute-start.6 = (bf16[256,256]{1,0:T(8,128)(2,1)S(1)}, bf16[256,256]{1,0:T(8,128)(2,1)S(1)}, u32[]{:S(2)}, u32[]{:S(2)}) collective-permute-start(bf16[256,256]{1,0:T(8,128)(2,1)S(1)} %get-tuple-element.11), channel_id=1, source_target_pairs={{0,16},{1,17},{2,18},{3,19},{4,20},{5,21},{6,22},{7,23},{8,24},{9,... | collective-permute-start | bytes 393224 | tf_op jit(solution)/shard_map/ppermute | solution.py:16
  78.2 15.9 %collective-permute-start.7 = (bf16[1024,256]{1,0:T(8,128)(2,1)S(1)}, bf16[1024,256]{1,0:T(8,128)(2,1)S(1)}, u32[]{:S(2)}, u32[]{:S(2)}) collective-permute-start(bf16[1024,256]{1,0:T(8,128)(2,1)S(1)} %get-tuple-element.7), channel_id=1, source_target_pairs={{4,0},{8,4},{12,8},{16,12},{20,16},{24,20},{28,24},{5,1},{9,5},{13... | collective-permute-start | bytes 1572872 | tf_op jit(solution)/shard_map/ppermute | solution.py:41
  80.1 26.0 %collective-permute-start.8 = (bf16[1024,256]{1,0:T(8,128)(2,1)S(1)}, bf16[1024,256]{1,0:T(8,128)(2,1)S(1)}, u32[]{:S(2)}, u32[]{:S(2)}) collective-permute-start(bf16[1024,256]{1,0:T(8,128)(2,1)S(1)} %get-tuple-element.8), channel_id=1, source_target_pairs={{0,4},{4,8},{8,12},{12,16},{16,20},{20,24},{24,28},{1,5},{5,9},{9,... | collective-permute-start | bytes 1572872 | tf_op jit(solution)/shard_map/ppermute | solution.py:41
  107.2 15.8 %collective-permute-start.10 = (bf16[1024,256]{1,0:T(8,128)(2,1)S(1)}, bf16[1024,256]{1,0:T(8,128)(2,1)S(1)}, u32[]{:S(2)}, u32[]{:S(2)}) collective-permute-start(bf16[1024,256]{1,0:T(8,128)(2,1)S(1)} %get-tuple-element.3), channel_id=1, source_target_pairs={{4,0},{8,4},{12,8},{16,12},{20,16},{24,20},{28,24},{5,1},{9,5},{13... | collective-permute-start | bytes 1572872 | tf_op jit(solution)/shard_map/ppermute | solution.py:31
  109.1 25.9 %collective-permute-start.9 = (bf16[1024,256]{1,0:T(8,128)(2,1)S(1)}, bf16[1024,256]{1,0:T(8,128)(2,1)S(1)}, u32[]{:S(2)}, u32[]{:S(2)}) collective-permute-start(bf16[1024,256]{1,0:T(8,128)(2,1)S(1)} %get-tuple-element.3), channel_id=1, source_target_pairs={{0,4},{4,8},{8,12},{12,16},{16,20},{20,24},{24,28},{1,5},{5,9},{9,... | collective-permute-start | bytes 1572872 | tf_op jit(solution)/shard_map/ppermute | solution.py:29
  143.6 4.9 %collective-permute-start.11 = (bf16[16,256]{1,0:T(8,128)(2,1)S(1)}, bf16[16,256]{1,0:T(8,128)(2,1)S(1)}, u32[]{:S(2)}, u32[]{:S(2)}) collective-permute-start(bf16[16,256]{1,0:T(8,128)(2,1)S(1)} %gather_fusion.3), channel_id=1, source_target_pairs={{0,31},{1,0},{2,1},{3,2},{4,3},{5,4},{6,5},{7,6},{8,7},{9,8},{10,9... | collective-permute-start | bytes 24584 | tf_op jit(solution)/shard_map/ppermute | solution.py:16
  148.6 4.4 %collective-permute-start.12 = (bf16[32,256]{1,0:T(8,128)(2,1)S(1)}, bf16[32,256]{1,0:T(8,128)(2,1)S(1)}, u32[]{:S(2)}, u32[]{:S(2)}) collective-permute-start(bf16[32,256]{1,0:T(8,128)(2,1)S(1)} %pad_maximum_fusion.7), channel_id=1, source_target_pairs={{0,30},{1,31},{2,0},{3,1},{4,2},{5,3},{6,4},{7,5},{8,6},{9,7},{10,... | collective-permute-start | bytes 49160 | tf_op jit(solution)/shard_map/ppermute | solution.py:16
  152.9 3.7 %collective-permute-start.13 = (bf16[64,256]{1,0:T(8,128)(2,1)S(1)}, bf16[64,256]{1,0:T(8,128)(2,1)S(1)}, u32[]{:S(2)}, u32[]{:S(2)}) collective-permute-start(bf16[64,256]{1,0:T(8,128)(2,1)S(1)} %pad_maximum_fusion.5), channel_id=1, source_target_pairs={{0,28},{1,29},{2,30},{3,31},{4,0},{5,1},{6,2},{7,3},{8,4},{9,5},{1... | collective-permute-start | bytes 98312 | tf_op jit(solution)/shard_map/ppermute | solution.py:16
  156.6 3.6 %collective-permute-start.14 = (bf16[128,256]{1,0:T(8,128)(2,1)S(1)}, bf16[128,256]{1,0:T(8,128)(2,1)S(1)}, u32[]{:S(2)}, u32[]{:S(2)}) collective-permute-start(bf16[128,256]{1,0:T(8,128)(2,1)S(1)} %pad_maximum_fusion.3), channel_id=1, source_target_pairs={{0,24},{1,25},{2,26},{3,27},{4,28},{5,29},{6,30},{7,31},{8,0},{9,1... | collective-permute-start | bytes 196616 | tf_op jit(solution)/shard_map/ppermute | solution.py:16
  160.2 8.8 %collective-permute-start.15 = (bf16[256,256]{1,0:T(8,128)(2,1)S(1)}, bf16[256,256]{1,0:T(8,128)(2,1)S(1)}, u32[]{:S(2)}, u32[]{:S(2)}) collective-permute-start(bf16[256,256]{1,0:T(8,128)(2,1)S(1)} %get-tuple-element.9), channel_id=1, source_target_pairs={{0,16},{1,17},{2,18},{3,19},{4,20},{5,21},{6,22},{7,23},{8,24},{9,... | collective-permute-start | bytes 393224 | tf_op jit(solution)/shard_map/ppermute | solution.py:16
  180.6 15.4 %collective-permute-start.16 = (bf16[1024,256]{1,0:T(8,128)(2,1)S(1)}, bf16[1024,256]{1,0:T(8,128)(2,1)S(1)}, u32[]{:S(2)}, u32[]{:S(2)}) collective-permute-start(bf16[1024,256]{1,0:T(8,128)(2,1)S(1)} %get-tuple-element.5), channel_id=1, source_target_pairs={{4,0},{8,4},{12,8},{16,12},{20,16},{24,20},{28,24},{5,1},{9,5},{13... | collective-permute-start | bytes 1572872 | tf_op jit(solution)/shard_map/ppermute | solution.py:41
  182.5 25.9 %collective-permute-start.17 = (bf16[1024,256]{1,0:T(8,128)(2,1)S(1)}, bf16[1024,256]{1,0:T(8,128)(2,1)S(1)}, u32[]{:S(2)}, u32[]{:S(2)}) collective-permute-start(bf16[1024,256]{1,0:T(8,128)(2,1)S(1)} %get-tuple-element.6), channel_id=1, source_target_pairs={{0,4},{4,8},{8,12},{12,16},{16,20},{20,24},{24,28},{1,5},{5,9},{9,... | collective-permute-start | bytes 1572872 | tf_op jit(solution)/shard_map/ppermute | solution.py:41
